TPU v7x, 32 devices: a whole 2x2x4 slice. The times are simulated.
32 devices in a mesh: parts: 2 (over y), filt: 4 (over z), space: 4 (over x, core).
Axes of the slice: x: 2, y: 2, z: 4, core: 2. Of those that a mesh axis runs over, the one named last changes fastest.
Arguments:
- volume: bfloat16 [512, 16, 8, 128], P('filt', ('parts', 'space')), parts along dimension 1, may hold values from -6 to 6
- weight: bfloat16 [512, 27, 512], P('filt'), may hold values from -0.0546875 to 0.0546875
- bias: float32 [512], P('filt'), may hold values from -3 to 3
- upstream: bfloat16 [512, 16, 8, 128], P('filt', ('parts', 'space')), parts along dimension 1, may hold values from -0.0625 to 0.0625
Outputs:
- features: bfloat16 [512, 16, 8, 128], P('filt', ('parts', 'space')), parts along dimension 1
- weight_grad: float32 [1024, 27, 512], P(('parts', 'filt')), parts along dimension 0
There are 2 independent parts, one for each index of `parts`. A program takes and returns all parts, laid end to end along the dimension named above; an argument that names none is the same for every part. Nothing has to cross between parts.
All inputs are finite; a program needn't handle non-finite values.
Results may differ from a plain program's by a relative error of at most 0.001.
Values may be sent and summed in bfloat16 or wider, within the bound.
No kernel may reach another device: no remote copies, remote signals or barrier semaphores. Data moves between devices by JAX's collectives and lax.ppermute only.
A program may use at most 128 MiB of HBM per device.

v0:
```python
import jax
import jax.numpy as jnp
from jax import lax
from jax.sharding import PartitionSpec as P


def padded(block, sides, width):
    for axis, dim in sides:
        count = lax.axis_size(axis)
        forward = [(i, i + 1) for i in range(count - 1)]
        backward = [(target, source) for source, target in forward]
        low = lax.ppermute(
            lax.slice_in_dim(block, block.shape[dim] - width, None, axis=dim), axis, forward
        )
        high = lax.ppermute(lax.slice_in_dim(block, 0, width, axis=dim), axis, backward)
        block = jnp.concatenate([low, block, high], axis=dim)
    return block


def convolve(slab, kernel):
    return lax.conv_general_dilated(
        slab[None],
        kernel,
        (1, 1, 1),
        [(0, 0), (1, 1), (1, 1)],
        dimension_numbers=("NCDHW", "OIDHW", "NCDHW"),
        preferred_element_type=jnp.float32,
    )[0]


def shifted_slopes(upstream):
    out_dev = upstream.shape[0]
    depth = upstream.shape[1]
    height = upstream.shape[2]
    length = upstream.shape[3]
    spread = jnp.pad(upstream, ((0, 0), (2, 2), (1, 1), (1, 1)))
    copies = []
    for tap in range(27):
        first = tap // 9
        second = tap // 3 % 3
        third = tap % 3
        copies.append(
            spread[
                :,
                2 - first : 4 - first + depth,
                2 - second : 2 - second + height,
                2 - third : 2 - third + length,
            ]
        )
    stacked = jnp.stack(copies, 1)
    return stacked.reshape(out_dev * 27, (depth + 2) * height * length)


def tap_grads(slab, slopes, out_dev):
    flat = slab.reshape(slab.shape[0], -1)
    product = lax.dot_general(
        slopes, flat, (((1,), (1,)), ((), ())), preferred_element_type=jnp.float32
    )
    return product.reshape(out_dev, 27, slab.shape[0])


def on_device(volume, weight, bias, upstream):
    out_dev = weight.shape[0]
    in_all = weight.shape[2]
    kernel = weight.reshape(out_dev, 3, 3, 3, in_all).transpose(0, 4, 1, 2, 3)
    slopes = shifted_slopes(upstream)
    whole = lax.all_gather(volume, "filt", axis=0, tiled=True)
    rimmed = padded(whole, (("space", 1),), 1)
    pre = convolve(rimmed, kernel)
    partial_grads = tap_grads(rimmed, slopes, out_dev)
    weight_grad = lax.psum(partial_grads, "space")
    pre = pre + bias[:, None, None, None]
    features = jnp.where(pre > 0, pre, 0.3 * pre).astype(jnp.bfloat16)
    return (features, weight_grad)


def solution(mesh):
    return jax.shard_map(
        on_device,
        mesh=mesh,
        in_specs=(
            P("filt", ("parts", "space"), None, None),
            P("filt", None, None),
            P("filt"),
            P("filt", ("parts", "space"), None, None),
        ),
        out_specs=(P("filt", ("parts", "space"), None, None), P(("parts", "filt"), None, None)),
        check_vma=False,
    )
```

profile of v0, /device:TPU:0, one launch (start us, length us, event | category | flops | bytes accessed | tf_op | source)
XLA Modules:
  0.0 254.6 jit_solution(8644923369791404062)
XLA Ops:
  7.2 2.1 copy.8
  9.4 1.2 copy.13
  10.6 1.3 fusion.19
  11.9 1.2 fusion.21
  13.1 1.3 fusion.23
  14.3 1.3 fusion.25
  15.6 1.1 fusion.27
  16.8 1.3 fusion.29
  18.1 1.3 fusion.31
  19.4 1.2 fusion.33
  20.5 1.4 fusion.35
  21.9 1.2 fusion.37
  23.1 1.1 fusion.39
  24.3 1.3 fusion.41
  25.6 1.4 fusion.43
  26.9 1.1 fusion.45
  28.1 1.3 fusion.47
  29.4 1.3 fusion.49
  30.6 1.1 fusion.51
  31.8 1.3 fusion.53
  33.1 1.3 fusion.55
  34.4 24.5 %all-gather.2.cloned.1.call-done = bf16[512,2,8,128]{3,0,2,1:T(8,128)(2,1)} async-done(((bf16[128,2,8,128]{3,0,2,1:T(8,128)(2,1)}), bf16[512,2,8,128]{3,0,2,1:T(8,128)(2,1)}) %all-gather.2.cloned.1.call-update) | async-done | bytes 2097168 | tf_op jit(solution)/shard_map/all_gather | solution.py:67
  58.8 1.7 fusion.76
  60.5 1.8 collective-permute-start
  62.3 2.2 fusion.57
  64.5 2.3 fusion.59
  66.8 1.3 collective-permute-start.1
  68.1 2.3 fusion.61
  70.4 2.2 fusion.63
  72.6 2.3 fusion.65
  75.0 2.4 fusion.67
  77.3 2.1 fusion.69
  79.5 2.3 fusion.71
  81.8 0.1 constant_dynamic-update-slice_fusion.2
  81.9 1.9 constant_dynamic-update-slice_fusion.1
  83.8 0.1 constant_dynamic-update-slice_fusion
  84.0 2.0 copy-done.2
  86.0 20.7 %fusion.10 = f32[128,27,512]{2,0,1:T(8,128)} fusion(bf16[128,27,4,8,128]{4,0,3,2,1:T(8,128)(2,1)} %fusion.71, bf16[512,4,8,128]{3,0,2,1:T(8,128)(2,1)S(1)} %constant_dynamic-update-slice_fusion), kind=kOutput, calls=%fused_computation.38 | convolution fusion | flops 14495514624 | bytes 39583744 | tf_op jit(solution)/shard_map/dot_general | solution.py:56
  106.7 8.0 %copy.18 = bf16[512,4,8,1,128]{0,2,4,1,3:T(8,128)(2,1)} copy(bf16[512,4,8,1,128]{4,0,2,1,3:T(8,128)(2,1)} %bitcast.144) | data formatting | bytes 8388608
  114.7 2.6 %pad.5.clone = bf16[512,4,8,1,136]{0,2,4,1,3:T(8,128)(2,1)S(1)} pad(bf16[512,4,8,1,128]{0,2,4,1,3:T(8,128)(2,1)} %copy.18, bf16[]{:T(256)} %constant.6.clone.1), padding=0_0x0_0x0_0x0_0x1_7 | pad | bytes 8650754 | tf_op jit(solution)/shard_map/broadcast_in_dim | solution.py:22
  117.3 1.7 copy.11
  119.1 0.1 slice.120
  119.2 16.9 %fusion.14 = f32[2,8,8,17,128]{4,2,3,1,0:T(8,128)S(1)} fusion(bf16[128,3,3,3,512]{4,0,3,2,1:T(8,128)(2,1)S(1)} %bitcast.142, bf16[512,4,8,1,7,2]{0,4,5,2,1,3:T(8,128)(2,1)S(1)} %slice.120, bf16[512,4,8,1,8,17]{0,4,5,2,1,3:T(8,128)(2,1)S(1)} %copy.11, pred[8,17]{0,1:T(8,128)(4,1)S(1)} %copy-done.4), kind=kOutput, calls=%fused_computation.40 | convolution fusion | flops 7074234368 | bytes 9568392 | tf_op jit(solution)/shard_map/conv_general_dilated | solution.py:21
  136.1 0.2 copy.12
  136.3 1.0 fusion.17
  137.3 2.4 copy.14
  139.7 100.7 %all-reduce.3.cloned.1.call-done = f32[128,27,512]{2,0,1:T(8,128)} async-done(((f32[128,27,512]{2,0,1:T(8,128)}), f32[128,27,512]{2,0,1:T(8,128)}) %all-reduce.3.cloned.1.call-update) | async-done | bytes 7077904 | tf_op jit(solution)/shard_map/psum | solution.py:71
  240.4 7.3 %copy.48 = f32[128,27,512]{2,0,1:T(8,128)} copy(f32[128,27,512]{2,0,1:T(8,128)} %all-reduce.3.cloned.1.call-done) | data formatting | bytes 14155776
  (15 shorter events, 0.1 us)
Async XLA Ops:
  7.2 112.0 %copy-start = (bf16[128,27,512]{2,0,1:T(8,128)(2,1)S(1)}, bf16[128,27,512]{2,0,1:T(8,128)(2,1)}, u32[]{:S(2)}) copy-start(bf16[128,27,512]{2,0,1:T(8,128)(2,1)} %param.5) | copy-start | bytes 10616836
  7.2 51.7 %all-gather.2.cloned.1.call-start = ((), (), s32[]{:S(2)}) async-start(), calls=%async_computation | async-start | bytes 2621440 | tf_op jit(solution)/shard_map/all_gather | solution.py:67
  9.4 231.0 %all-reduce.3.cloned.1.call-start = ((), (), s32[]{:S(2)}) async-start(), calls=%async_computation.1 | async-start | bytes 14155776 | tf_op jit(solution)/shard_map/psum | solution.py:71
  10.6 22.5 %copy-start.1 = (bf16[128,2,8,128]{3,0,2,1:T(8,128)(2,1)}, bf16[128,2,8,128]{3,0,2,1:T(8,128)(2,1)S(1)}, u32[]{:S(2)}) copy-start(bf16[128,2,8,128]{3,0,2,1:T(8,128)(2,1)S(1)} %copy.13) | copy-start | bytes 1572868
  60.5 21.2 %collective-permute-start = (bf16[512,1,8,128]{3,0,2,1:T(8,128)(2,1)S(1)}, bf16[512,1,8,128]{3,0,2,1:T(8,128)(2,1)S(1)}, u32[]{:S(2)}, u32[]{:S(2)}) collective-permute-start(bf16[512,1,8,128]{3,0,2,1:T(8,128)(2,1)S(1)} %get-tuple-element.5), channel_id=1, source_target_pairs={{0,1},{1,2},{2,3},{4,5},{5,6},{6,7},{8,9},{9,10},{10,11},{12,13},{... | collective-permute-start | bytes 3145736 | tf_op jit(solution)/shard_map/ppermute | solution.py:12
  66.8 17.0 %collective-permute-start.1 = (bf16[512,1,8,128]{3,0,2,1:T(8,128)(2,1)S(1)}, bf16[512,1,8,128]{3,0,2,1:T(8,128)(2,1)S(1)}, u32[]{:S(2)}, u32[]{:S(2)}) collective-permute-start(bf16[512,1,8,128]{3,0,2,1:T(8,128)(2,1)S(1)} %get-tuple-element.4), channel_id=1, source_target_pairs={{1,0},{2,1},{3,2},{5,4},{6,5},{7,6},{9,8},{10,9},{11,10},{13,12},{... | collective-permute-start | bytes 3145736 | tf_op jit(solution)/shard_map/ppermute | solution.py:15
  83.9 2.0 copy-start.2
  106.6 12.6 %copy-start.4 = (pred[8,17]{0,1:T(8,128)(4,1)S(1)}, pred[8,17]{0,1:T(8,128)(4,1)}, u32[]{:S(2)}) copy-start(pred[8,17]{0,1:T(8,128)(4,1)} %constant.15) | copy-start | bytes 412
  119.2 17.1 %copy-start.3 = (f32[128]{0:T(128)S(1)}, f32[128]{0:T(128)}, u32[]{:S(2)}) copy-start(f32[128]{0:T(128)} %param.6) | copy-start | bytes 1540
Sparse Core Ops, SparseCore 0:
  10.2 48.6 all-gather.1
  106.8 133.5 all-reduce.2
where the time goes:
time: 255 us
  waiting for transfers between devices  125 us (49%)
  local copies, waits for them, and re-layouts  73.5 us (29%)
  matrix products  37.5 us (15%)
  between operations  14.2 us (6%)
  starting transfers between devices  3.13 us (1%)
    psum x1, waiting for transfers between devices, on_device(): weight_grad = lax.psum(partial_grads, 'space')  101 us
    unnamed x43, local copies, waits for them, and re-layouts  64.7 us
    all_gather x1, waiting for transfers between devices, on_device(): whole = lax.all_gather(volume, 'filt', axis=0, tiled=True)  24.5 us
    dot_general x1, matrix products, tap_grads(): lax.dot_general(slopes, flat, (((1,), (1,)), ((), ())), preferred_element...  20.7 us
    conv_general_dilated x1, matrix products, convolve(): lax.conv_general_dilated(slab[None], kernel, (1, 1, 1), [(0, 0), (1, 1),...  16.9 us
  transfers between devices with their start and end apart: 4, of which 2 were waited for; matrix products, arithmetic and copies ran while one was open for 31% of the time, Pallas kernels for 0%

commit v1 on v0

--- a/solution.py
+++ b/solution.py
@@ -2,6 +2,19 @@
 import jax.numpy as jnp
 from jax import lax
 from jax.sharding import PartitionSpec as P
+
+
+def gather_around(x, axis, dim):
+    ways = lax.axis_size(axis)
+    up = [(d, (d + 1) % ways) for d in range(ways)]
+    down = [(d, (d - 1) % ways) for d in range(ways)]
+    earlier, later = ([x], [x])
+    for _ in range(ways // 2):
+        earlier.append(lax.ppermute(earlier[-1], axis, up))
+    for _ in range((ways - 1) // 2):
+        later.append(lax.ppermute(later[-1], axis, down))
+    line = jnp.concatenate([*earlier[::-1], *later[1:]], axis=dim)
+    return jnp.roll(line, (lax.axis_index(axis) - ways // 2) * x.shape[dim], axis=dim)
 
 
 def padded(block, sides, width):
@@ -64,7 +77,7 @@
     in_all = weight.shape[2]
     kernel = weight.reshape(out_dev, 3, 3, 3, in_all).transpose(0, 4, 1, 2, 3)
     slopes = shifted_slopes(upstream)
-    whole = lax.all_gather(volume, "filt", axis=0, tiled=True)
+    whole = gather_around(volume, "filt", 0)
     rimmed = padded(whole, (("space", 1),), 1)
     pre = convolve(rimmed, kernel)
     partial_grads = tap_grads(rimmed, slopes, out_dev)

time: 255 us -> 245 us (0.961)
  local copies, waits for them, and re-layouts: 73.5 us -> 63.7 us
  waiting for transfers between devices: 125 us -> 116 us
  starting transfers between devices: 3.13 us -> 7.92 us
  other arithmetic: 0.96 us -> 4.76 us
    all_gather x1 -> x0, waiting for transfers between devices: 24.5 us -> none  [on_device(): whole = lax.all_gather(volume, 'filt', axis=0, tiled=True)]
    ppermute x0 -> x3, waiting for transfers between devices: none -> 16.4 us  [the longest x2 16.4 us: gather_around(): earlier.append(lax.ppermute(earlier[-1], axis, up))]
    unnamed x43 -> x56, local copies, waits for them, and re-layouts: 64.7 us -> 56.4 us
    ppermute x0 -> x3, starting transfers between devices: none -> 5.05 us  [the longest x2 3.03 us: gather_around(): earlier.append(lax.ppermute(earlier[-1], axis, up))]
    broadcast_in_dim x0 -> x1, other arithmetic: none -> 3.8 us  [convolve(): slab[None]]
  transfers between devices with their start and end apart: 4 -> 6, of which waited for: 2 -> 3; matrix products, arithmetic and copies ran while one was open for 31% -> 24% of each run, Pallas kernels for 0% -> 0%
where the time goes in v1:
time: 245 us
  waiting for transfers between devices  116 us (47%)
  local copies, waits for them, and re-layouts  63.7 us (26%)
  matrix products  37.5 us (15%)
  between operations  14.4 us (6%)
  starting transfers between devices  7.92 us (3%)
  other arithmetic  4.76 us (2%)
    psum x1, waiting for transfers between devices, on_device(): weight_grad = lax.psum(partial_grads, 'space')  99.8 us
    unnamed x56, local copies, waits for them, and re-layouts  56.4 us
    dot_general x1, matrix products, tap_grads(): lax.dot_general(slopes, flat, (((1,), (1,)), ((), ())), preferred_element...  20.6 us
    conv_general_dilated x1, matrix products, convolve(): lax.conv_general_dilated(slab[None], kernel, (1, 1, 1), [(0, 0), (1, 1),...  16.9 us
    ppermute x2, waiting for transfers between devices, gather_around(): earlier.append(lax.ppermute(earlier[-1], axis, up))  16.4 us
  transfers between devices with their start and end apart: 6, of which 3 were waited for; matrix products, arithmetic and copies ran while one was open for 24% of the time, Pallas kernels for 0%

profile of v1, /device:TPU:0, one launch (start us, length us, event | category | flops | bytes accessed | tf_op | source)
XLA Modules:
  0.0 244.5 jit_solution(12869868688648636536)
XLA Ops:
  7.2 2.1 copy.11
  9.3 3.0 %collective-permute-start = (bf16[128,2,8,128]{3,0,2,1:T(8,128)(2,1)}, bf16[128,2,8,128]{3,0,2,1:T(8,128)(2,1)}, u32[]{:S(2)}, u32[]{:S(2)}) collective-permute-start(bf16[128,2,8,128]{3,0,2,1:T(8,128)(2,1)} %copy.11), channel_id=1, source_target_pairs={{0,4},{4,8},{8,12},{12,0},{1,5},{5,9},{9,13},{13,1},{2,6},{6,10},{... | collective-permute-start | bytes 1572872 | tf_op jit(solution)/shard_map/ppermute | solution.py:13
  12.4 2.0 collective-permute-start.2
  14.4 1.2 copy.19
  16.1 0.5 fusion.24
  16.6 0.5 fusion.26
  17.4 0.5 fusion.30
  17.9 0.5 fusion.32
  18.6 0.5 fusion.36
  19.1 0.5 fusion.38
  19.8 0.5 fusion.42
  20.3 0.5 fusion.44
  21.0 0.5 fusion.48
  21.5 0.5 fusion.50
  22.0 5.5 %collective-permute-done = bf16[128,2,8,128]{3,0,2,1:T(8,128)(2,1)} collective-permute-done((bf16[128,2,8,128]{3,0,2,1:T(8,128)(2,1)}, bf16[128,2,8,128]{3,0,2,1:T(8,128)(2,1)}, u32[]{:S(2)}, u32[]{:S(2)}) %collective-permute-start) | collective-permute-done | bytes 524320 | tf_op jit(solution)/shard_map/ppermute | solution.py:13
  27.8 0.5 fusion.54
  28.2 0.5 fusion.56
  29.0 9.3 %copy-done.6 = bf16[128,27,4,8,128]{4,0,3,2,1:T(8,128)(2,1)} copy-done((bf16[128,27,4,8,128]{4,0,3,2,1:T(8,128)(2,1)}, bf16[128,27,4,8,128]{4,0,3,2,1:T(8,128)(2,1)S(1)}, u32[]{:S(2)}) %copy-start.6) | copy-done | bytes 28311576
  38.3 10.8 %collective-permute-done.1 = bf16[128,2,8,128]{3,0,2,1:T(8,128)(2,1)} collective-permute-done((bf16[128,2,8,128]{3,0,2,1:T(8,128)(2,1)}, bf16[128,2,8,128]{3,0,2,1:T(8,128)(2,1)}, u32[]{:S(2)}, u32[]{:S(2)}) %collective-permute-start.1) | collective-permute-done | bytes 524320 | tf_op jit(solution)/shard_map/ppermute | solution.py:13
  49.1 1.1 constant_dynamic-update-slice_fusion.7
  50.2 1.1 constant_dynamic-update-slice_fusion.6
  51.4 1.2 constant_dynamic-update-slice_fusion.5
  52.6 1.1 constant_dynamic-update-slice_fusion.4
  53.7 1.1 constant_dynamic-update-slice_fusion.3
  54.9 1.1 constant_dynamic-update-slice_fusion.2
  56.0 1.2 constant_dynamic-update-slice_fusion.1
  57.2 1.1 constant_dynamic-update-slice_fusion
  58.5 1.4 collective-permute-start.3
  59.9 1.5 collective-permute-start.4
  61.4 1.3 fusion.60
  62.7 1.3 fusion.62
  64.0 1.2 fusion.64
  65.1 1.3 fusion.66
  66.5 1.4 fusion.68
  67.8 1.1 fusion.70
  68.9 1.3 fusion.72
  70.4 1.4 copy-done.3
  72.1 1.0 copy-done.5
  73.1 20.6 %fusion.10 = f32[128,27,512]{2,0,1:T(8,128)} fusion(bf16[128,27,4,8,128]{4,0,3,2,1:T(8,128)(2,1)} %fusion.72, bf16[512,1,8,128]{3,0,2,1:T(8,128)(2,1)S(1)} %collective-permute-done.4, bf16[512,2,8,128]{3,0,2,1:T(8,128)(2,1)S(1)} %constant_dynamic-slice_fusion.2, bf16[512,1,8,128]{3,0,2,1:T(8,128)(2,1)S(1)} %collective-permute-done.3), kind=kOutput, calls=%fused_computation.39 | convolution fusion | flops 14499708928 | bytes 39583744 | tf_op jit(solution)/shard_map/dot_general | solution.py:69
  93.7 3.8 %fusion.14 = bf16[512,4,8,1,128]{4,0,2,1,3:T(8,128)(2,1)} fusion(bf16[512,1,8,128]{3,0,2,1:T(8,128)(2,1)} %copy-done.5, bf16[512,2,8,128]{3,0,2,1:T(8,128)(2,1)} %copy-done.3, bf16[512,1,8,128]{3,0,2,1:T(8,128)(2,1)} %copy-done.4), kind=kLoop, calls=%fused_computation.41 | loop fusion | flops 4194304 | bytes 8388608 | tf_op jit(solution)/shard_map/broadcast_in_dim | solution.py:35
  97.5 8.1 %copy.24 = bf16[512,4,8,1,128]{0,2,4,1,3:T(8,128)(2,1)} copy(bf16[512,4,8,1,128]{4,0,2,1,3:T(8,128)(2,1)} %fusion.14) | data formatting | bytes 8388608
  105.6 2.5 %pad.5.clone = bf16[512,4,8,1,136]{0,2,4,1,3:T(8,128)(2,1)S(1)} pad(bf16[512,4,8,1,128]{0,2,4,1,3:T(8,128)(2,1)} %copy.24, bf16[]{:T(256)} %constant.38.clone.1), padding=0_0x0_0x0_0x0_0x1_7 | pad | bytes 8650754 | tf_op jit(solution)/shard_map/broadcast_in_dim | solution.py:35
  108.2 1.7 copy.17
  110.1 16.9 %fusion.15 = f32[2,8,8,17,128]{4,2,3,1,0:T(8,128)S(1)} fusion(bf16[128,3,3,3,512]{4,0,3,2,1:T(8,128)(2,1)S(1)} %bitcast.143, bf16[512,4,8,1,7,2]{0,4,5,2,1,3:T(8,128)(2,1)S(1)} %slice.118, bf16[512,4,8,1,8,17]{0,4,5,2,1,3:T(8,128)(2,1)S(1)} %copy.17, pred[8,17]{0,1:T(8,128)(4,1)S(1)} %copy-done.8), kind=kOutput, calls=%fused_computation.42 | convolution fusion | flops 7074234368 | bytes 9568392 | tf_op jit(solution)/shard_map/conv_general_dilated | solution.py:34
  127.2 1.0 fusion.18
  128.2 2.4 copy.20
  130.5 99.8 %all-reduce.3.cloned.1.call-done = f32[128,27,512]{2,0,1:T(8,128)} async-done(((f32[128,27,512]{2,0,1:T(8,128)}), f32[128,27,512]{2,0,1:T(8,128)}) %all-reduce.3.cloned.1.call-update) | async-done | bytes 7077904 | tf_op jit(solution)/shard_map/psum | solution.py:84
  230.4 7.3 %copy.61 = f32[128,27,512]{2,0,1:T(8,128)} copy(f32[128,27,512]{2,0,1:T(8,128)} %all-reduce.3.cloned.1.call-done) | data formatting | bytes 14155776
  (33 shorter events, 3.1 us)
Async XLA Ops:
  7.2 102.9 %copy-start = (bf16[128,27,512]{2,0,1:T(8,128)(2,1)S(1)}, bf16[128,27,512]{2,0,1:T(8,128)(2,1)}, u32[]{:S(2)}) copy-start(bf16[128,27,512]{2,0,1:T(8,128)(2,1)} %param.5) | copy-start | bytes 10616836
  7.2 223.2 %all-reduce.3.cloned.1.call-start = ((), (), s32[]{:S(2)}) async-start(), calls=%async_computation | async-start | bytes 14155776 | tf_op jit(solution)/shard_map/psum | solution.py:84
  9.3 18.2 %collective-permute-start = (bf16[128,2,8,128]{3,0,2,1:T(8,128)(2,1)}, bf16[128,2,8,128]{3,0,2,1:T(8,128)(2,1)}, u32[]{:S(2)}, u32[]{:S(2)}) collective-permute-start(bf16[128,2,8,128]{3,0,2,1:T(8,128)(2,1)} %copy.11), channel_id=1, source_target_pairs={{0,4},{4,8},{8,12},{12,0},{1,5},{5,9},{9,13},{13,1},{2,6},{6,10},{... | collective-permute-start | bytes 1572872 | tf_op jit(solution)/shard_map/ppermute | solution.py:13
  12.4 40.2 %collective-permute-start.2 = (bf16[128,2,8,128]{3,0,2,1:T(8,128)(2,1)}, bf16[128,2,8,128]{3,0,2,1:T(8,128)(2,1)}, u32[]{:S(2)}, u32[]{:S(2)}) collective-permute-start(bf16[128,2,8,128]{3,0,2,1:T(8,128)(2,1)} %copy.11), channel_id=1, source_target_pairs={{0,12},{4,0},{8,4},{12,8},{1,13},{5,1},{9,5},{13,9},{2,14},{6,2},{... | collective-permute-start | bytes 1572872 | tf_op jit(solution)/shard_map/ppermute | solution.py:15
  15.6 13.1 %copy-start.1 = (bf16[128,2,8,128]{3,0,2,1:T(8,128)(2,1)}, bf16[128,2,8,128]{3,0,2,1:T(8,128)(2,1)S(1)}, u32[]{:S(2)}) copy-start(bf16[128,2,8,128]{3,0,2,1:T(8,128)(2,1)S(1)} %copy.19) | copy-start | bytes 1572868
  27.5 21.6 %collective-permute-start.1 = (bf16[128,2,8,128]{3,0,2,1:T(8,128)(2,1)}, bf16[128,2,8,128]{3,0,2,1:T(8,128)(2,1)}, u32[]{:S(2)}, u32[]{:S(2)}) collective-permute-start(bf16[128,2,8,128]{3,0,2,1:T(8,128)(2,1)} %collective-permute-done), channel_id=1, source_target_pairs={{0,4},{4,8},{8,12},{12,0},{1,5},{5,9},{9,13},{13,1},{2,6},{6,10},{... | collective-permute-start | bytes 1572872 | tf_op jit(solution)/shard_map/ppermute | solution.py:13
  29.0 9.3 %copy-start.6 = (bf16[128,27,4,8,128]{4,0,3,2,1:T(8,128)(2,1)}, bf16[128,27,4,8,128]{4,0,3,2,1:T(8,128)(2,1)S(1)}, u32[]{:S(2)}) copy-start(bf16[128,27,4,8,128]{4,0,3,2,1:T(8,128)(2,1)S(1)} %fusion.58) | copy-start | bytes 84934656
  38.3 23.1 %copy-start.2 = (bf16[128,2,8,128]{3,0,2,1:T(8,128)(2,1)S(1)}, bf16[128,2,8,128]{3,0,2,1:T(8,128)(2,1)}, u32[]{:S(2)}) copy-start(bf16[128,2,8,128]{3,0,2,1:T(8,128)(2,1)} %copy-done.1) | copy-start | bytes 1572868
  58.5 11.8 %collective-permute-start.3 = (bf16[512,1,8,128]{3,0,2,1:T(8,128)(2,1)S(1)}, bf16[512,1,8,128]{3,0,2,1:T(8,128)(2,1)S(1)}, u32[]{:S(2)}, u32[]{:S(2)}) collective-permute-start(bf16[512,1,8,128]{3,0,2,1:T(8,128)(2,1)S(1)} %get-tuple-element.4), channel_id=1, source_target_pairs={{0,1},{1,2},{2,3},{4,5},{5,6},{6,7},{8,9},{9,10},{10,11},{12,13},{... | collective-permute-start | bytes 3145736 | tf_op jit(solution)/shard_map/ppermute | solution.py:25
  59.9 10.5 %collective-permute-start.4 = (bf16[512,1,8,128]{3,0,2,1:T(8,128)(2,1)S(1)}, bf16[512,1,8,128]{3,0,2,1:T(8,128)(2,1)S(1)}, u32[]{:S(2)}, u32[]{:S(2)}) collective-permute-start(bf16[512,1,8,128]{3,0,2,1:T(8,128)(2,1)S(1)} %get-tuple-element.5), channel_id=1, source_target_pairs={{1,0},{2,1},{3,2},{5,4},{6,5},{7,6},{9,8},{10,9},{11,10},{13,12},{... | collective-permute-start | bytes 3145736 | tf_op jit(solution)/shard_map/ppermute | solution.py:28
  70.4 1.5 copy-start.3
  70.4 1.7 copy-start.4
  72.1 1.0 copy-start.5
  108.2 1.9 copy-start.8
  110.1 17.2 %copy-start.7 = (f32[128]{0:T(128)S(1)}, f32[128]{0:T(128)}, u32[]{:S(2)}) copy-start(f32[128]{0:T(128)} %param.6) | copy-start | bytes 1540
Sparse Core Ops, SparseCore 0:
  93.8 136.4 all-reduce.2
